TPU v7x, 256 devices: a whole 4x4x8 slice. The times are simulated.
256 devices in a mesh: row: 4 (over y), col: 4 (over x), dp: 16 (over z, core).
Axes of the slice: x: 4, y: 4, z: 8, core: 2. Of those that a mesh axis runs over, the one named last changes fastest.
Arguments:
- hidden_states: bfloat16 [16384, 1536], P(('dp', 'row'), 'col'), may hold values from -18 to 18
- w_query: bfloat16 [1536, 1536], P('col', 'row'), may hold values from -0.102062073 to 0.102062073
- w_key_value: bfloat16 [1536, 512], P('col'), may hold values from -0.102062073 to 0.102062073
- adapter_down: bfloat16 [1024, 1536, 16], P('dp', 'col'), may hold values from -0.15625 to 0.15625
- adapter_up: bfloat16 [1024, 16, 1536], P('dp', None, 'row'), may hold values from -1.5 to 1.5
- req_lengths: int32 [16, 8], replicated, may hold values from 1 to 160, 960 in all within a row
- req_adapter: int32 [16, 8], replicated, may hold values from 0 to 1023, as said below
Outputs:
- attention: bfloat16 [16384, 1536], P(('dp', 'col'), 'row')
- kv_cache: bfloat16 [16384, 512], P(('dp', 'col'))
Inputs may be any that keep to these rules, and one draw needn't show every extreme that they name: `req_lengths`: the lengths of one block sum to 960, and each block has a request of exactly 160 tokens. `req_adapter`: adapters k * 64 to (k + 1) * 64 - 1 are those of index k of dp; the requests of one block use adapters of one index of dp at most 1 times, and some index of dp is used exactly that often by every block.
All inputs are finite; a program needn't handle non-finite values.
Results may differ from a plain program's by a relative error of at most 0.0072.
Values may be sent and summed in bfloat16 or wider, within the bound.
No kernel may reach another device: no remote copies, remote signals or barrier semaphores. Data moves between devices by JAX's collectives and lax.ppermute only.
A program may use at most 128 MiB of HBM per device.

v0:
```python
import math
import jax
import jax.numpy as jnp
from jax import lax
from jax.sharding import PartitionSpec as P

HEAD_DIM = 128
MOST_LEN = 160
masked_score = -1e30


def block_layout(lengths_row, block_len):
    prefix_len = block_len - jnp.sum(lengths_row)
    ends_at = jnp.cumsum(lengths_row) + prefix_len
    starts = ends_at - lengths_row
    positions = jnp.arange(block_len, dtype=jnp.int32)
    segment = jnp.sum((positions[:, None] >= starts[None, :]).astype(jnp.int32), axis=1)
    return (starts, segment, positions)


def slot_numbers(holders):
    request_total = holders.shape[0]
    ordering = jnp.arange(request_total, dtype=jnp.int32)
    earlier = ordering[None, :] < ordering[:, None]
    same_holder = holders[:, None] == holders[None, :]
    return jnp.sum((earlier & same_holder).astype(jnp.int32), axis=1)


def make_attend(query_rows, segment, first_row, kv_group, head_size, kv_half):
    own_rows = query_rows.shape[0]
    heads_here = query_rows.shape[1] // head_size
    query_heads = query_rows.reshape(own_rows, heads_here, head_size)
    query_pos = first_row + jnp.arange(own_rows, dtype=jnp.int32)
    query_seg = lax.dynamic_slice_in_dim(segment, first_row, own_rows, 0)
    score_scale = 1.0 / math.sqrt(head_size)

    def attend(state_in, key_block, key_start):
        running_max, running_sum, running_out = state_in
        block_size = key_block.shape[0]
        key_rows = lax.dynamic_slice_in_dim(key_block, kv_group * head_size, head_size, 1)
        values = lax.dynamic_slice_in_dim(key_block, kv_half + kv_group * head_size, head_size, 1)
        key_pos = jnp.arange(block_size, dtype=jnp.int32)
        allowed = (key_pos[None, :] <= query_pos[:, None]) & (
            (segment[None, :] == query_seg[:, None]) | (segment[None, :] == 0)
        )
        scores = (
            jnp.einsum("qhd,kd->hqk", query_heads, key_rows, preferred_element_type=jnp.float32)
            * score_scale
        )
        scores = jnp.where(allowed[None], scores, masked_score)
        new_max = jnp.maximum(running_max, jnp.max(scores, axis=2))
        weights = jnp.where(allowed[None], jnp.exp(scores - new_max[:, :, None]), 0.0)
        running_sum = jnp.sum(weights, axis=2)
        running_out = jnp.einsum(
            "hqk,kd->hqd", weights.astype(jnp.bfloat16), values, preferred_element_type=jnp.float32
        )
        return (new_max, running_sum, running_out)

    initial = (
        jnp.full((heads_here, own_rows), masked_score, jnp.float32),
        jnp.zeros((heads_here, own_rows), jnp.float32),
        jnp.zeros((heads_here, own_rows, head_size), jnp.float32),
    )
    return (attend, initial)


def body(hidden_states, w_query, w_key_value, adapter_down, adapter_up, req_lengths, req_adapter):
    dp_size = lax.axis_size("dp")
    block_index = lax.axis_index("dp")
    col_index = lax.axis_index("col")
    row_index = lax.axis_index("row")
    gathered = lax.all_gather(hidden_states, "row", axis=0, tiled=True)
    block_len = gathered.shape[0]
    query_cols = w_query.shape[1]
    kv_cols = w_key_value.shape[1]
    kv_half = kv_cols // 2
    head_size = HEAD_DIM
    heads_here = query_cols // head_size
    heads_total = heads_here * lax.axis_size("row")
    kv_heads = kv_half // head_size
    kv_group = row_index * heads_here // (heads_total // kv_heads)
    own_rows = block_len // lax.axis_size("col")
    first_row = col_index * own_rows
    held_sets = adapter_down.shape[0]
    width_here = adapter_down.shape[1]
    rank_size = adapter_down.shape[2]
    lengths_row = req_lengths[block_index]
    adapters_row = req_adapter[block_index]
    requests = lengths_row.shape[0]
    starts, segment, positions = block_layout(lengths_row, block_len)
    request_of = jnp.clip(segment - 1, 0, requests - 1)
    in_request = segment > 0
    holders = adapters_row // held_sets
    slot_of = slot_numbers(holders)
    per_holder = (requests + dp_size - 1) // dp_size
    longest = MOST_LEN
    target_ids = jnp.arange(dp_size, dtype=jnp.int32)[:, None, None]
    slot_ids = jnp.arange(per_holder, dtype=jnp.int32)[None, :, None]
    pairing = (holders[None, None, :] == target_ids) & (slot_of[None, None, :] == slot_ids)
    pair_int = pairing.astype(jnp.int32)
    slot_start = jnp.sum(pair_int * starts[None, None, :], axis=2)
    slot_len = jnp.sum(pair_int * lengths_row[None, None, :], axis=2)
    slot_adapter = jnp.where(
        jnp.any(pairing, axis=2),
        jnp.sum(pair_int * (adapters_row % held_sets)[None, None, :], axis=2),
        -1,
    )
    offsets = jnp.arange(longest, dtype=jnp.int32)
    token_at = slot_start[:, :, None] + offsets[None, None, :]
    live_rows = offsets[None, None, :] < slot_len[:, :, None]
    outgoing = jnp.where(
        live_rows[..., None],
        gathered[jnp.clip(token_at, 0, block_len - 1)],
        jnp.zeros((), gathered.dtype),
    )
    flat_down = jnp.transpose(adapter_down, (1, 0, 2)).reshape(width_here, held_sets * rank_size)
    flat_up = adapter_up.reshape(held_sets * rank_size, query_cols).astype(jnp.float32)
    rank_owner = jnp.arange(held_sets * rank_size, dtype=jnp.int32) // rank_size
    sent_rows = lax.all_to_all(outgoing, "dp", split_axis=0, concat_axis=0, tiled=True)
    sent_ids = lax.all_to_all(
        slot_adapter.astype(jnp.bfloat16), "dp", split_axis=0, concat_axis=0, tiled=True
    )
    reduced = jnp.einsum("nkld,da->nkla", sent_rows, flat_down, preferred_element_type=jnp.float32)
    kept_cols = rank_owner[None, None, :] == sent_ids.astype(jnp.int32)[:, :, None]
    reduced = jnp.where(kept_cols[:, :, None, :], reduced, 0.0)
    adapter_part = jnp.einsum("nkla,af->nklf", reduced, flat_up, precision=lax.Precision.HIGHEST)
    returned = lax.all_to_all(adapter_part, "dp", split_axis=0, concat_axis=0, tiled=True)
    flat_index = (holders[request_of] * per_holder + slot_of[request_of]) * longest + jnp.clip(
        positions - starts[request_of], 0, longest - 1
    )
    adapter_term = returned.reshape(-1, query_cols)[flat_index]
    adapter_term = jnp.where(in_request[:, None], adapter_term, 0.0)
    both_weights = jnp.concatenate([w_query, w_key_value], axis=1)
    partial_value = jnp.dot(gathered, both_weights, preferred_element_type=jnp.float32)
    summed = lax.psum_scatter(
        partial_value
        + jnp.concatenate(
            [adapter_term, jnp.zeros((own_rows * lax.axis_size("col"), kv_cols), jnp.float32)],
            axis=1,
        ),
        "col",
        scatter_dimension=0,
        tiled=True,
    )
    query_rows = summed[:, :query_cols].astype(jnp.bfloat16)
    kv_cache = summed[:, query_cols:].astype(jnp.bfloat16)
    attend, initial = make_attend(query_rows, segment, first_row, kv_group, head_size, kv_half)
    running_max, running_sum, running_out = attend(
        initial, lax.all_gather(kv_cache, "col", axis=0, tiled=True), jnp.int32(0)
    )
    attention = (running_out / running_sum[:, :, None]).astype(jnp.bfloat16)
    attention = jnp.transpose(attention, (1, 0, 2)).reshape(own_rows, query_cols)
    return (attention, kv_cache)


def solution(mesh):
    return jax.shard_map(
        body,
        mesh=mesh,
        in_specs=(
            P(("dp", "row"), "col"),
            P("col", "row"),
            P("col", None),
            P("dp", "col", None),
            P("dp", None, "row"),
            P(),
            P(),
        ),
        out_specs=(P(("dp", "col"), "row"), P(("dp", "col"), None)),
        check_vma=False,
    )
```

profile of v0, /device:TPU:8, one launch (start us, length us, event | category | flops | bytes accessed | tf_op | source)
XLA Modules:
  0.0 303.4 jit_solution(6985747026854632109)
XLA Ops:
  7.2 1.5 fusion.34
  11.0 0.7 copy.46
  11.7 8.6 %all-to-all-start = ((bf16[16,1,1]{2,1,0:T(2,128)(2,1)}), bf16[16,1,1]{2,1,0:T(2,128)(2,1)}, u32[]{:S(2)}, u32[]{:S(2)}) async-start(bf16[16,1,1]{2,1,0:T(2,128)(2,1)} %copy.46), calls=%async_computation | async-start | bytes 16384 | tf_op jit(solution)/shard_map/all_to_all | solution.py:120
  20.5 14.9 %all_gather.6 = bf16[1024,384]{1,0:T(8,128)(2,1)S(1)} all-gather(bf16[256,384]{1,0:T(8,128)(2,1)} %param.7), channel_id=1, replica_groups=mesh['row'=4,'col'=4,'dp'=16] {'row'}, dimensions={0}, use_global_device_ids=true | all-gather | bytes 983040 | tf_op jit(solution)/shard_map/all_gather | solution.py:72
  35.5 7.5 %gather_fusion = bf16[2560,384]{1,0:T(8,128)(2,1)S(1)} fusion(bf16[1024,384]{1,0:T(8,128)(2,1)S(1)} %all_gather.6, s32[3072]{0:T(1024)S(1)} %pad_clamp_fusion), kind=kCustom, calls=%fused_computation | custom fusion | bytes 3942400 | tf_op jit(solution)/shard_map/gather | solution.py:113
  43.0 1.5 broadcast_select_fusion
  44.5 7.0 %all-to-all-start.1 = ((bf16[16,1,160,384]{3,2,1,0:T(8,128)(2,1)}), bf16[16,1,160,384]{3,2,1,0:T(8,128)(2,1)S(1)}, u32[]{:S(2)}, u32[]{:S(2)}) async-start(bf16[16,1,160,384]{3,2,1,0:T(8,128)(2,1)} %broadcast_select_fusion), calls=%async_computation.1 | async-start | bytes 3932160 | tf_op jit(solution)/shard_map/all_to_all | solution.py:119
  51.5 1.1 convert_reduce_fusion.1
  52.7 45.2 %all-to-all-done.1 = bf16[16,1,160,384]{3,2,1,0:T(8,128)(2,1)S(1)} async-done(((bf16[16,1,160,384]{3,2,1,0:T(8,128)(2,1)}), bf16[16,1,160,384]{3,2,1,0:T(8,128)(2,1)S(1)}, u32[]{:S(2)}, u32[]{:S(2)}) %all-to-all-start.1) | async-done | bytes 1966112 | tf_op jit(solution)/shard_map/all_to_all | solution.py:119
  97.9 3.0 fusion.10
  100.9 10.3 %fusion.7 = f32[16,1,160,384]{3,2,1,0:T(8,128)} fusion(bf16[1024,384,1]{1,0,2:T(8,128)(2,1)S(1)} %bitcast.109, f32[16,160,1024]{2,1,0:T(8,128)S(1)} %fusion.10, pred[16,1024]{1,0:T(8,128)(4,1)S(1)} %broadcast_compare_fusion), kind=kOutput, calls=%fused_computation.12 | convolution fusion | flops 12082216960 | bytes 15220736 | tf_op jit(solution)/shard_map/nkla,af->nklf/dot_general | solution.py:126
  111.2 4.8 %all-to-all-start.2 = ((f32[16,1,160,384]{3,2,1,0:T(8,128)}), f32[16,1,160,384]{3,2,1,0:T(8,128)}, u32[]{:S(2)}, u32[]{:S(2)}) async-start(f32[16,1,160,384]{3,2,1,0:T(8,128)} %fusion.7), calls=%async_computation.2 | async-start | bytes 7864320 | tf_op jit(solution)/shard_map/all_to_all | solution.py:127
  116.2 0.7 fusion.52
  117.6 0.7 fusion.53
  118.4 4.1 %select_select_fusion.2 = s32[1024,1]{0,1:T(1,128)S(1)} fusion(s32[]{:T(128)} %bitcast.20, s32[]{:T(128)} %bitcast.21, s32[]{:T(128)} %bitcast.22, s32[]{:T(128)} %bitcast.23, s32[]{:T(128)} %bitcast.24, s32[]{:T(128)} %bitcast.26, s32[]{:T(128)} %bitcast.25, s32[1024,1]{0,1:T(1,128)S(1)} %bitcast.113), kind=kLoop, calls=%fused_computation.56 | loop fusion | flops 15360 | bytes 8220 | tf_op jit(solution)/shard_map/gather | solution.py:128
  122.5 9.0 %select_select_fusion = (s32[1024,1]{0,1:T(1,128)S(1)}, s32[1024,1]{0,1:T(1,128)S(1)}) fusion(s32[]{:T(128)} %bitcast.39, s32[]{:T(128)} %bitcast.40, s32[]{:T(128)} %bitcast.41, s32[]{:T(128)} %bitcast.42, s32[]{:T(128)} %bitcast.43, s32[]{:T(128)} %bitcast.45, s32[]{:T(128)} %bitcast.44, s32[1024,1]{0,1:T(1,128)S(1)} %bitcast.114, s32[]{:T(128)} %bitcast.35, ...), kind=kLoop, calls=%fused_computation.54 | loop fusion | flops 21504 | bytes 12344 | tf_op jit(solution)/shard_map/gather | solution.py:129
  131.6 1.9 broadcast_select_fusion.2
  133.5 71.2 %all-to-all-done.2 = f32[16,1,160,384]{3,2,1,0:T(8,128)} async-done(((f32[16,1,160,384]{3,2,1,0:T(8,128)}), f32[16,1,160,384]{3,2,1,0:T(8,128)}, u32[]{:S(2)}, u32[]{:S(2)}) %all-to-all-start.2) | async-done | bytes 3932192 | tf_op jit(solution)/shard_map/all_to_all | solution.py:127
  204.7 7.1 %gather_fusion.1 = f32[1024,384]{1,0:T(8,128)} fusion(f32[2560,384]{1,0:T(8,128)} %bitcast.17, s32[1024]{0:T(1024)S(1)} %broadcast_clamp_fusion), kind=kCustom, calls=%fused_computation.1 | custom fusion | bytes 3149824 | tf_op jit(solution)/shard_map/gather | solution.py:131
  211.8 1.9 copy.50
  213.9 0.8 copy-done.3
  214.7 3.0 bitcast_add_fusion
  217.8 43.7 %reduce-scatter.2.cloned.1.call-done = f32[256,896]{0,1:T(8,128)} async-done(((f32[1024,896]{0,1:T(8,128)}), f32[256,896]{0,1:T(8,128)}) %reduce-scatter.2.cloned.1.call-update) | async-done | bytes 917520 | tf_op jit(solution)/shard_map/reduce_scatter | solution.py:135
  261.5 1.2 convert.5
  262.7 0.7 slice.41
  263.6 0.8 fusion.18
  264.4 1.8 copy.55
  266.2 25.1 %all-gather.2.cloned.1.call-done = bf16[1024,512]{0,1:T(8,128)(2,1)} async-done(((bf16[256,512]{0,1:T(8,128)(2,1)}), bf16[1024,512]{0,1:T(8,128)(2,1)}) %all-gather.2.cloned.1.call-update) | async-done | bytes 1048592 | tf_op jit(solution)/shard_map/all_gather | solution.py:149
  291.3 1.7 fusion.4
  293.0 0.8 fusion.5
  293.8 1.9 fusion.22
  295.8 0.8 copy.54
  (60 shorter events, 3.4 us)
Async XLA Ops:
  7.2 90.7 %copy-start = (bf16[64,384,16]{1,2,0:T(8,128)(2,1)S(1)}, bf16[64,384,16]{1,2,0:T(8,128)(2,1)}, u32[]{:S(2)}) copy-start(bf16[64,384,16]{1,2,0:T(8,128)(2,1)} %param.10) | copy-start | bytes 2359300
  8.8 11.6 %copy-start.10 = (s32[1,8]{1,0:T(1,128)}, s32[1,8]{1,0:T(1,128)S(1)}, u32[]{:S(2)}) copy-start(s32[1,8]{1,0:T(1,128)S(1)} %copy.62) | copy-start | bytes 100
  8.9 11.4 %copy-start.12 = (s32[8,1]{0,1:T(1,128)}, s32[8,1]{0,1:T(1,128)S(1)}, u32[]{:S(2)}) copy-start(s32[8,1]{0,1:T(1,128)S(1)} %reduce-window.4) | copy-start | bytes 100
  9.0 11.4 %copy-start.6 = (s32[8]{0:T(128)}, s32[8]{0:T(128)S(1)}, u32[]{:S(2)}) copy-start(s32[8]{0:T(128)S(1)} %get-tuple-element.49) | copy-start | bytes 100
  9.1 0.5 copy-start.8
  10.4 0.5 copy-start.4
  11.7 32.8 %all-to-all-start = ((bf16[16,1,1]{2,1,0:T(2,128)(2,1)}), bf16[16,1,1]{2,1,0:T(2,128)(2,1)}, u32[]{:S(2)}, u32[]{:S(2)}) async-start(bf16[16,1,1]{2,1,0:T(2,128)(2,1)} %copy.46), calls=%async_computation | async-start | bytes 16384 | tf_op jit(solution)/shard_map/all_to_all | solution.py:120
  44.5 53.4 %all-to-all-start.1 = ((bf16[16,1,160,384]{3,2,1,0:T(8,128)(2,1)}), bf16[16,1,160,384]{3,2,1,0:T(8,128)(2,1)S(1)}, u32[]{:S(2)}, u32[]{:S(2)}) async-start(bf16[16,1,160,384]{3,2,1,0:T(8,128)(2,1)} %broadcast_select_fusion), calls=%async_computation.1 | async-start | bytes 3932160 | tf_op jit(solution)/shard_map/all_to_all | solution.py:119
  97.9 3.0 copy-start.1
  111.2 5.0 %copy-start.5 = (s32[8]{0:T(128)S(1)}, s32[8]{0:T(128)}, u32[]{:S(2)}) copy-start(s32[8]{0:T(128)} %copy-done.4) | copy-start | bytes 100
  111.2 5.7 %copy-start.9 = (s32[8]{0:T(128)S(1)}, s32[8]{0:T(128)}, u32[]{:S(2)}) copy-start(s32[8]{0:T(128)} %copy-done.8) | copy-start | bytes 100
  111.2 6.4 %copy-start.7 = (s32[8]{0:T(128)S(1)}, s32[8]{0:T(128)}, u32[]{:S(2)}) copy-start(s32[8]{0:T(128)} %copy-done.6) | copy-start | bytes 100
  111.2 7.1 %copy-start.11 = (s32[1,8]{1,0:T(1,128)S(1)}, s32[1,8]{1,0:T(1,128)}, u32[]{:S(2)}) copy-start(s32[1,8]{1,0:T(1,128)} %copy-done.10) | copy-start | bytes 100
  111.2 7.1 %copy-start.13 = (s32[8,1]{0,1:T(1,128)S(1)}, s32[8,1]{0,1:T(1,128)}, u32[]{:S(2)}) copy-start(s32[8,1]{0,1:T(1,128)} %copy-done.12) | copy-start | bytes 100
  111.2 93.5 %all-to-all-start.2 = ((f32[16,1,160,384]{3,2,1,0:T(8,128)}), f32[16,1,160,384]{3,2,1,0:T(8,128)}, u32[]{:S(2)}, u32[]{:S(2)}) async-start(f32[16,1,160,384]{3,2,1,0:T(8,128)} %fusion.7), calls=%async_computation.2 | async-start | bytes 7864320 | tf_op jit(solution)/shard_map/all_to_all | solution.py:127
  116.0 145.5 %reduce-scatter.2.cloned.1.call-start = ((), (), s32[]{:S(2)}) async-start(), calls=%async_computation.4 | async-start | bytes 4587520 | tf_op jit(solution)/shard_map/reduce_scatter | solution.py:135
  211.8 2.1 copy-start.2
  213.8 1.0 copy-start.3
  217.7 73.6 %all-gather.2.cloned.1.call-start = ((), (), s32[]{:S(2)}) async-start(), calls=%async_computation.5 | async-start | bytes 1310720 | tf_op jit(solution)/shard_map/all_gather | solution.py:149
Sparse Core Ops, SparseCore 0:
  217.8 43.6 reduce-scatter.1
  263.6 27.6 all-gather.1
where the time goes:
time: 304 us; the launch traced here: 303 us
  waiting for transfers between devices  185 us (61%)
  local copies, waits for them, and re-layouts  24.7 us (8%)
  other arithmetic  23.1 us (8%)
  starting transfers between devices  20.6 us (7%)
  matrix products  19.9 us (7%)
  between operations  15 us (5%)
  blocking collectives  14.9 us (5%)
    all_to_all x1, waiting for transfers between devices, body(): lax.all_to_all(adapter_part, 'dp', split_axis=0, concat_axis=0, tiled=True)  71.2 us
    all_to_all x1, waiting for transfers between devices, body(): lax.all_to_all(outgoing, 'dp', split_axis=0, concat_axis=0, tiled=True)  45.2 us
    reduce_scatter x1, waiting for transfers between devices, body(): lax.psum_scatter(partial_value + jnp.concatenate([adapter_term, jnp.zeros...  43.7 us
    all_gather x1, waiting for transfers between devices, body(): lax.all_gather(kv_cache, 'col', axis=0, tiled=True)  25.1 us
    all_gather x1, blocking collectives, body(): gathered = lax.all_gather(hidden_states, 'row', axis=0, tiled=True)  14.9 us
    gather x2, other arithmetic, body(): starts[request_of]  10.9 us
    dot_general x1, matrix products, body(): jnp.einsum('nkla,af->nklf', reduced, flat_up, precision=lax.Precision.HIG...  10.3 us
    gather x2, local copies, waits for them, and re-layouts, body(): adapter_term = returned.reshape(-1, query_cols)[flat_index]  9.02 us
  transfers between devices with their start and end apart: 5, of which 4 were waited for; matrix products, arithmetic and copies ran while one was open for 10% of the time, Pallas kernels for 0%

commit v1 on v0

--- a/solution.py
+++ b/solution.py
@@ -146,7 +146,11 @@
     kv_cache = summed[:, query_cols:].astype(jnp.bfloat16)
     attend, initial = make_attend(query_rows, segment, first_row, kv_group, head_size, kv_half)
     running_max, running_sum, running_out = attend(
-        initial, lax.all_gather(kv_cache, "col", axis=0, tiled=True), jnp.int32(0)
+        initial,
+        jnp.concatenate(
+            lax.all_to_all(jnp.stack([kv_cache] * lax.axis_size("col")), "col", 0, 0), axis=0
+        ),
+        jnp.int32(0),
     )
     attention = (running_out / running_sum[:, :, None]).astype(jnp.bfloat16)
     attention = jnp.transpose(attention, (1, 0, 2)).reshape(own_rows, query_cols)

time: 304 us -> 294 us (0.967)
  waiting for transfers between devices: 185 us -> 175 us
  starting transfers between devices: 20.6 us -> 24.1 us
    all_gather x1 -> x0, waiting for transfers between devices: 25.1 us -> none  [body(): lax.all_gather(kv_cache, 'col', axis=0, tiled=True)]
    all_to_all x0 -> x1, waiting for transfers between devices: none -> 14.3 us  [body(): lax.all_to_all(jnp.stack([kv_cache] * lax.axis_size('col')), 'col', 0, 0)]
    all_to_all x0 -> x1, starting transfers between devices: none -> 3.51 us  [body(): lax.all_to_all(jnp.stack([kv_cache] * lax.axis_size('col')), 'col', 0, 0)]
where the time goes in v1:
time: 294 us; the launch traced here: 293 us
  waiting for transfers between devices  175 us (60%)
  starting transfers between devices  24.1 us (8%)
  local copies, waits for them, and re-layouts  23.4 us (8%)
  other arithmetic  23.1 us (8%)
  matrix products  17.9 us (6%)
  between operations  15.1 us (5%)
  blocking collectives  14.9 us (5%)
    all_to_all x1, waiting for transfers between devices, body(): lax.all_to_all(adapter_part, 'dp', split_axis=0, concat_axis=0, tiled=True)  71.2 us
    all_to_all x1, waiting for transfers between devices, body(): lax.all_to_all(outgoing, 'dp', split_axis=0, concat_axis=0, tiled=True)  45.2 us
    reduce_scatter x1, waiting for transfers between devices, body(): lax.psum_scatter(partial_value + jnp.concatenate([adapter_term, jnp.zeros...  43.8 us
    all_gather x1, blocking collectives, body(): gathered = lax.all_gather(hidden_states, 'row', axis=0, tiled=True)  14.9 us
    all_to_all x1, waiting for transfers between devices, body(): lax.all_to_all(jnp.stack([kv_cache] * lax.axis_size('col')), 'col', 0, 0)  14.3 us
    gather x2, other arithmetic, body(): starts[request_of]  10.9 us
    dot_general x1, matrix products, body(): jnp.einsum('nkla,af->nklf', reduced, flat_up, precision=lax.Precision.HIG...  10.3 us
    gather x2, local copies, waits for them, and re-layouts, body(): adapter_term = returned.reshape(-1, query_cols)[flat_index]  9.02 us
  transfers between devices with their start and end apart: 5, of which 4 were waited for; matrix products, arithmetic and copies ran while one was open for 10% of the time, Pallas kernels for 0%

profile of v1, /device:TPU:8, one launch (start us, length us, event | category | flops | bytes accessed | tf_op | source)
XLA Modules:
  0.0 292.9 jit_solution(10576740022863681527)
XLA Ops:
  7.2 1.5 fusion.34
  11.0 0.7 copy.50
  11.7 8.6 %all-to-all-start = ((bf16[16,1,1]{2,1,0:T(2,128)(2,1)}), bf16[16,1,1]{2,1,0:T(2,128)(2,1)}, u32[]{:S(2)}, u32[]{:S(2)}) async-start(bf16[16,1,1]{2,1,0:T(2,128)(2,1)} %copy.50), calls=%async_computation | async-start | bytes 16384 | tf_op jit(solution)/shard_map/all_to_all | solution.py:120
  20.5 14.9 %all_gather.3 = bf16[1024,384]{1,0:T(8,128)(2,1)S(1)} all-gather(bf16[256,384]{1,0:T(8,128)(2,1)} %param.7), channel_id=1, replica_groups=mesh['row'=4,'col'=4,'dp'=16] {'row'}, dimensions={0}, use_global_device_ids=true | all-gather | bytes 983040 | tf_op jit(solution)/shard_map/all_gather | solution.py:72
  35.5 7.5 %gather_fusion = bf16[2560,384]{1,0:T(8,128)(2,1)S(1)} fusion(bf16[1024,384]{1,0:T(8,128)(2,1)S(1)} %all_gather.3, s32[3072]{0:T(1024)S(1)} %pad_clamp_fusion), kind=kCustom, calls=%fused_computation | custom fusion | bytes 3942400 | tf_op jit(solution)/shard_map/gather | solution.py:113
  43.0 1.5 broadcast_select_fusion
  44.5 7.0 %all-to-all-start.1 = ((bf16[16,1,160,384]{3,2,1,0:T(8,128)(2,1)}), bf16[16,1,160,384]{3,2,1,0:T(8,128)(2,1)S(1)}, u32[]{:S(2)}, u32[]{:S(2)}) async-start(bf16[16,1,160,384]{3,2,1,0:T(8,128)(2,1)} %broadcast_select_fusion), calls=%async_computation.1 | async-start | bytes 3932160 | tf_op jit(solution)/shard_map/all_to_all | solution.py:119
  51.5 1.1 convert_reduce_fusion.1
  52.7 45.2 %all-to-all-done.1 = bf16[16,1,160,384]{3,2,1,0:T(8,128)(2,1)S(1)} async-done(((bf16[16,1,160,384]{3,2,1,0:T(8,128)(2,1)}), bf16[16,1,160,384]{3,2,1,0:T(8,128)(2,1)S(1)}, u32[]{:S(2)}, u32[]{:S(2)}) %all-to-all-start.1) | async-done | bytes 1966112 | tf_op jit(solution)/shard_map/all_to_all | solution.py:119
  97.9 3.0 %fusion.10 = f32[16,160,1024]{2,1,0:T(8,128)S(1)} fusion(bf16[384,1024,1]{0,1,2:T(8,128)(2,1)S(1)} %bitcast.108, bf16[16,1,160,384]{3,2,1,0:T(8,128)(2,1)S(1)} %all-to-all-done.1), kind=kOutput, calls=%fused_computation.13 | convolution fusion | flops 2013265920 | bytes 13238272 | tf_op jit(solution)/shard_map/nkld,da->nkla/dot_general | solution.py:123
  100.9 10.3 %fusion.7 = f32[16,1,160,384]{3,2,1,0:T(8,128)} fusion(bf16[1024,384,1]{1,0,2:T(8,128)(2,1)S(1)} %bitcast.112, f32[16,160,1024]{2,1,0:T(8,128)S(1)} %fusion.10, pred[16,1024]{1,0:T(8,128)(4,1)S(1)} %broadcast_compare_fusion), kind=kOutput, calls=%fused_computation.12 | convolution fusion | flops 12082216960 | bytes 15220736 | tf_op jit(solution)/shard_map/nkla,af->nklf/dot_general | solution.py:126
  111.2 4.8 %all-to-all-start.2 = ((f32[16,1,160,384]{3,2,1,0:T(8,128)}), f32[16,1,160,384]{3,2,1,0:T(8,128)}, u32[]{:S(2)}, u32[]{:S(2)}) async-start(f32[16,1,160,384]{3,2,1,0:T(8,128)} %fusion.7), calls=%async_computation.2 | async-start | bytes 7864320 | tf_op jit(solution)/shard_map/all_to_all | solution.py:127
  116.2 0.7 fusion.52
  117.6 0.7 fusion.53
  118.4 4.1 %select_select_fusion.2 = s32[1024,1]{0,1:T(1,128)S(1)} fusion(s32[]{:T(128)} %bitcast.20, s32[]{:T(128)} %bitcast.21, s32[]{:T(128)} %bitcast.22, s32[]{:T(128)} %bitcast.23, s32[]{:T(128)} %bitcast.24, s32[]{:T(128)} %bitcast.26, s32[]{:T(128)} %bitcast.25, s32[1024,1]{0,1:T(1,128)S(1)} %bitcast.116), kind=kLoop, calls=%fused_computation.56 | loop fusion | flops 15360 | bytes 8220 | tf_op jit(solution)/shard_map/gather | solution.py:128
  122.5 9.0 %select_select_fusion = (s32[1024,1]{0,1:T(1,128)S(1)}, s32[1024,1]{0,1:T(1,128)S(1)}) fusion(s32[]{:T(128)} %bitcast.39, s32[]{:T(128)} %bitcast.40, s32[]{:T(128)} %bitcast.41, s32[]{:T(128)} %bitcast.42, s32[]{:T(128)} %bitcast.43, s32[]{:T(128)} %bitcast.45, s32[]{:T(128)} %bitcast.44, s32[1024,1]{0,1:T(1,128)S(1)} %bitcast.117, s32[]{:T(128)} %bitcast.35, ...), kind=kLoop, calls=%fused_computation.54 | loop fusion | flops 21504 | bytes 12344 | tf_op jit(solution)/shard_map/gather | solution.py:129
  131.6 1.9 broadcast_select_fusion.2
  133.5 71.2 %all-to-all-done.2 = f32[16,1,160,384]{3,2,1,0:T(8,128)} async-done(((f32[16,1,160,384]{3,2,1,0:T(8,128)}), f32[16,1,160,384]{3,2,1,0:T(8,128)}, u32[]{:S(2)}, u32[]{:S(2)}) %all-to-all-start.2) | async-done | bytes 3932192 | tf_op jit(solution)/shard_map/all_to_all | solution.py:127
  204.7 7.1 %gather_fusion.1 = f32[1024,384]{1,0:T(8,128)} fusion(f32[2560,384]{1,0:T(8,128)} %bitcast.17, s32[1024]{0:T(1024)S(1)} %broadcast_clamp_fusion), kind=kCustom, calls=%fused_computation.1 | custom fusion | bytes 3149824 | tf_op jit(solution)/shard_map/gather | solution.py:131
  211.8 1.9 copy.54
  213.9 0.8 copy-done.4
  214.7 3.0 %bitcast_add_fusion = f32[1024,896]{0,1:T(8,128)} fusion(f32[1024,384]{0,1:T(8,128)S(1)} %broadcast_select_fusion.1, bf16[1024,384]{1,0:T(8,128)(2,1)S(1)} %all_gather.3, bf16[384,512]{1,0:T(8,128)(2,1)S(1)} %copy-done.3, bf16[384,384]{1,0:T(8,128)(2,1)S(1)} %copy-done.4), kind=kOutput, calls=%fused_computation.6 | convolution fusion | flops 706936832 | bytes 6717440 | tf_op jit(solution)/shard_map/dot_general | solution.py:134
  217.7 43.8 %reduce-scatter.2.cloned.1.call-done = f32[256,896]{0,1:T(8,128)} async-done(((f32[1024,896]{0,1:T(8,128)}), f32[256,896]{0,1:T(8,128)}) %reduce-scatter.2.cloned.1.call-update) | async-done | bytes 917520 | tf_op jit(solution)/shard_map/reduce_scatter | solution.py:135
  261.5 1.2 convert.5
  262.9 1.1 stack.2
  264.0 3.5 %all-to-all-start.3 = ((bf16[4,256,512]{2,1,0:T(8,128)(2,1)}), bf16[4,256,512]{2,1,0:T(8,128)(2,1)S(1)}, u32[]{:S(2)}, u32[]{:S(2)}) async-start(bf16[4,256,512]{2,1,0:T(8,128)(2,1)} %stack.2), calls=%async_computation.4 | async-start | bytes 2097152 | tf_op jit(solution)/shard_map/all_to_all | solution.py:151
  267.6 0.8 fusion.18
  268.4 14.3 %all-to-all-done.3 = bf16[4,256,512]{2,1,0:T(8,128)(2,1)S(1)} async-done(((bf16[4,256,512]{2,1,0:T(8,128)(2,1)}), bf16[4,256,512]{2,1,0:T(8,128)(2,1)S(1)}, u32[]{:S(2)}, u32[]{:S(2)}) %all-to-all-start.3) | async-done | bytes 1048608 | tf_op jit(solution)/shard_map/all_to_all | solution.py:151
  282.8 0.7 fusion.4
  283.5 0.8 fusion.5
  284.3 1.0 fusion.22
  285.3 0.8 copy.59
  (62 shorter events, 3.5 us)
Async XLA Ops:
  7.2 90.7 %copy-start = (bf16[64,384,16]{1,2,0:T(8,128)(2,1)S(1)}, bf16[64,384,16]{1,2,0:T(8,128)(2,1)}, u32[]{:S(2)}) copy-start(bf16[64,384,16]{1,2,0:T(8,128)(2,1)} %param.10) | copy-start | bytes 2359300
  8.8 11.6 %copy-start.11 = (s32[1,8]{1,0:T(1,128)}, s32[1,8]{1,0:T(1,128)S(1)}, u32[]{:S(2)}) copy-start(s32[1,8]{1,0:T(1,128)S(1)} %copy.67) | copy-start | bytes 100
  8.9 11.4 %copy-start.13 = (s32[8,1]{0,1:T(1,128)}, s32[8,1]{0,1:T(1,128)S(1)}, u32[]{:S(2)}) copy-start(s32[8,1]{0,1:T(1,128)S(1)} %reduce-window.4) | copy-start | bytes 100
  9.0 11.4 %copy-start.7 = (s32[8]{0:T(128)}, s32[8]{0:T(128)S(1)}, u32[]{:S(2)}) copy-start(s32[8]{0:T(128)S(1)} %get-tuple-element.49) | copy-start | bytes 100
  9.1 0.5 copy-start.9
  10.4 0.5 copy-start.5
  11.7 32.8 %all-to-all-start = ((bf16[16,1,1]{2,1,0:T(2,128)(2,1)}), bf16[16,1,1]{2,1,0:T(2,128)(2,1)}, u32[]{:S(2)}, u32[]{:S(2)}) async-start(bf16[16,1,1]{2,1,0:T(2,128)(2,1)} %copy.50), calls=%async_computation | async-start | bytes 16384 | tf_op jit(solution)/shard_map/all_to_all | solution.py:120
  44.5 53.4 %all-to-all-start.1 = ((bf16[16,1,160,384]{3,2,1,0:T(8,128)(2,1)}), bf16[16,1,160,384]{3,2,1,0:T(8,128)(2,1)S(1)}, u32[]{:S(2)}, u32[]{:S(2)}) async-start(bf16[16,1,160,384]{3,2,1,0:T(8,128)(2,1)} %broadcast_select_fusion), calls=%async_computation.1 | async-start | bytes 3932160 | tf_op jit(solution)/shard_map/all_to_all | solution.py:119
  97.9 3.0 %copy-start.2 = (bf16[64,16,384]{2,1,0:T(8,128)(2,1)S(1)}, bf16[64,16,384]{2,1,0:T(8,128)(2,1)}, u32[]{:S(2)}) copy-start(bf16[64,16,384]{2,1,0:T(8,128)(2,1)} %param.11) | copy-start | bytes 2359300
  111.2 5.0 %copy-start.6 = (s32[8]{0:T(128)S(1)}, s32[8]{0:T(128)}, u32[]{:S(2)}) copy-start(s32[8]{0:T(128)} %copy-done.5) | copy-start | bytes 100
  111.2 5.7 %copy-start.10 = (s32[8]{0:T(128)S(1)}, s32[8]{0:T(128)}, u32[]{:S(2)}) copy-start(s32[8]{0:T(128)} %copy-done.9) | copy-start | bytes 100
  111.2 6.4 %copy-start.8 = (s32[8]{0:T(128)S(1)}, s32[8]{0:T(128)}, u32[]{:S(2)}) copy-start(s32[8]{0:T(128)} %copy-done.7) | copy-start | bytes 100
  111.2 7.1 %copy-start.12 = (s32[1,8]{1,0:T(1,128)S(1)}, s32[1,8]{1,0:T(1,128)}, u32[]{:S(2)}) copy-start(s32[1,8]{1,0:T(1,128)} %copy-done.11) | copy-start | bytes 100
  111.2 7.1 %copy-start.14 = (s32[8,1]{0,1:T(1,128)S(1)}, s32[8,1]{0,1:T(1,128)}, u32[]{:S(2)}) copy-start(s32[8,1]{0,1:T(1,128)} %copy-done.13) | copy-start | bytes 100
  111.2 93.5 %all-to-all-start.2 = ((f32[16,1,160,384]{3,2,1,0:T(8,128)}), f32[16,1,160,384]{3,2,1,0:T(8,128)}, u32[]{:S(2)}, u32[]{:S(2)}) async-start(f32[16,1,160,384]{3,2,1,0:T(8,128)} %fusion.7), calls=%async_computation.2 | async-start | bytes 7864320 | tf_op jit(solution)/shard_map/all_to_all | solution.py:127
  116.0 145.5 %reduce-scatter.2.cloned.1.call-start = ((), (), s32[]{:S(2)}) async-start(), calls=%async_computation.5 | async-start | bytes 4587520 | tf_op jit(solution)/shard_map/reduce_scatter | solution.py:135
  211.8 2.1 copy-start.3
  213.8 1.0 copy-start.4
  262.9 20.6 %copy-start.1 = (bf16[256,512]{1,0:T(8,128)(2,1)}, bf16[256,512]{1,0:T(8,128)(2,1)S(1)}, u32[]{:S(2)}) copy-start(bf16[256,512]{1,0:T(8,128)(2,1)S(1)} %copy.55) | copy-start | bytes 786436
  264.0 18.8 %all-to-all-start.3 = ((bf16[4,256,512]{2,1,0:T(8,128)(2,1)}), bf16[4,256,512]{2,1,0:T(8,128)(2,1)S(1)}, u32[]{:S(2)}, u32[]{:S(2)}) async-start(bf16[4,256,512]{2,1,0:T(8,128)(2,1)} %stack.2), calls=%async_computation.4 | async-start | bytes 2097152 | tf_op jit(solution)/shard_map/all_to_all | solution.py:151
Sparse Core Ops, SparseCore 0:
  217.8 43.6 reduce-scatter.1
